TPU v7x, 512 devices: a whole 4x4x16 slice. The times are simulated.
512 devices in a mesh: section: 32 (over z, core), blk: 16 (over y, x).
Axes of the slice: x: 4, y: 4, z: 16, core: 2. Of those that a mesh axis runs over, the one named last changes fastest.
Arguments:
- held_input: bfloat16 [32, 5120, 128], P('section', 'blk'), may hold values from -6 to 6
- fresh_input: bfloat16 [5120, 128], P('blk'), may hold values from -6 to 6
- stashed: bfloat16 [32, 2, 5120, 128], P('section', None, 'blk'), may hold values from -6 to 6
- held_grad: bfloat16 [32, 5120, 128], P('section', 'blk'), may hold values from -6 to 6
- fresh_grad: bfloat16 [5120, 128], P('blk'), may hold values from -6 to 6
- first_up: bfloat16 [32, 2, 128, 6400], P('section', None, 'blk'), may hold values from -1 to 1
- second_up: bfloat16 [32, 2, 160, 16384], P('section', None, 'blk'), may hold values from -0.5 to 0.5
- first_down: bfloat16 [32, 160, 16384], P('section', 'blk'), may hold values from -0.5 to 0.5
- second_down: bfloat16 [32, 128, 6400], P('section', 'blk'), may hold values from -0.5 to 0.5
Outputs:
- passed_output: bfloat16 [32, 5120, 128], P('section', 'blk')
- passed_grad: bfloat16 [32, 5120, 128], P('section', 'blk')
- grad_first_up: bfloat16 [32, 2, 128, 6400], P('section', None, 'blk')
- grad_second_up: bfloat16 [32, 2, 160, 16384], P('section', None, 'blk')
- grad_first_down: bfloat16 [32, 160, 16384], P('section', 'blk')
- grad_second_down: bfloat16 [32, 128, 6400], P('section', 'blk')
All inputs are finite; a program needn't handle non-finite values.
Results may differ from a plain program's by a relative error of at most 0.0095.
Values may be sent and summed in bfloat16 or wider, within the bound.
No kernel may reach another device: no remote copies, remote signals or barrier semaphores. Data moves between devices by JAX's collectives and lax.ppermute only.
A program may use at most 64 MiB of HBM per device.

v0:
```python
import math
import jax
import jax.numpy as jnp
from jax import lax
from jax.sharding import PartitionSpec as P

BLOCK = 128
FIRST_BLOCKS = 128
FIRST_IN = 40
SECOND_BLOCKS = 160
TICKS = 2


def from_behind(value, axis, by):
    length = lax.axis_size(axis)
    pairs = [(i, i + by) for i in range(length) if 0 <= i + by < length]
    return lax.ppermute(value, axis, pairs)


def to_blocks(pieces):
    return lax.all_to_all(pieces, "blk", split_axis=2, concat_axis=1, tiled=True)


def to_features(pieces):
    return lax.all_to_all(pieces, "blk", split_axis=2, concat_axis=1, tiled=True)


def first_half(values, up_first):
    return jnp.einsum(
        "pqt,gpqr->gprt", values, up_first, preferred_element_type=jnp.float32
    ).astype(jnp.bfloat16)


def middle(spread, up_second, down_first):
    mixed = jnp.einsum("gprt,grpo->grot", spread, up_second, preferred_element_type=jnp.float32)
    hidden = (jax.nn.silu(mixed[0]) * mixed[1]).astype(jnp.bfloat16)
    lowered = jnp.einsum(
        "rot,rop->rpt", hidden, down_first, preferred_element_type=jnp.float32
    ).astype(jnp.bfloat16)
    return (mixed, hidden, lowered)


def last_half(values, lowered, down_second):
    added = jnp.einsum("rpt,prq->pqt", lowered, down_second, preferred_element_type=jnp.float32)
    return (values.astype(jnp.float32) + added).astype(jnp.bfloat16)


def backward_middle(mixed, grad_lowered, up_second, down_first):
    grad_hidden = jnp.einsum(
        "prt,rop->rot", grad_lowered, down_first, preferred_element_type=jnp.float32
    )
    sigmoid_gate = jax.nn.sigmoid(mixed[0])
    slope = sigmoid_gate * (1.0 + mixed[0] * (1.0 - sigmoid_gate))
    grad_mixed = jnp.stack(
        [grad_hidden * mixed[1] * slope, grad_hidden * mixed[0] * sigmoid_gate]
    ).astype(jnp.bfloat16)
    grad_spread = jnp.einsum(
        "grot,grpo->grpt", grad_mixed, up_second, preferred_element_type=jnp.float32
    ).astype(jnp.bfloat16)
    return (grad_mixed, grad_spread)


def shards(
    held_input,
    fresh_input,
    stashed,
    held_grad,
    fresh_grad,
    first_up,
    second_up,
    first_down,
    second_down,
):
    feature_blocks = first_up.shape[2]
    hidden_blocks = second_up.shape[2]
    tokens = held_input.shape[2]
    up_first = first_up[0].reshape(2, feature_blocks, FIRST_IN, SECOND_BLOCKS)
    up_second = second_up[0].reshape(2, hidden_blocks, FIRST_BLOCKS, BLOCK)
    down_first = first_down[0].reshape(hidden_blocks, BLOCK, FIRST_BLOCKS)
    down_second = second_down[0].reshape(feature_blocks, SECOND_BLOCKS, FIRST_IN)
    inputs = held_input[0].reshape(feature_blocks, FIRST_IN, tokens)
    grads = held_grad[0].reshape(feature_blocks, FIRST_IN, tokens)
    section_pos = lax.axis_index("section")
    last_section = lax.axis_size("section") - 1
    total_first_up = jnp.zeros(up_first.shape, jnp.float32)
    total_second_up = jnp.zeros(up_second.shape, jnp.float32)
    total_first_down = jnp.zeros(down_first.shape, jnp.float32)
    total_second_down = jnp.zeros(down_second.shape, jnp.float32)
    outputs = inputs
    backward = grads
    for tick_index in range(TICKS):
        stash_view = stashed[0, tick_index].reshape(feature_blocks, FIRST_IN, tokens)
        grad_lowered = jnp.einsum(
            "pqt,prq->prt", grads, down_second, preferred_element_type=jnp.float32
        ).astype(jnp.bfloat16)
        spread = to_blocks(first_half(inputs, up_first))
        mixed, hidden, lowered = middle(spread, up_second, down_first)
        outputs = last_half(inputs, to_features(lowered[None])[0], down_second)
        spread_stash = to_blocks(first_half(stash_view, up_first))
        mixed_stash, hidden_stash, lowered_stash = middle(spread_stash, up_second, down_first)
        lowered_back = to_features(lowered_stash[None])[0]
        grad_arrived = to_blocks(grad_lowered[None])[0]
        grad_mixed, grad_spread = backward_middle(mixed_stash, grad_arrived, up_second, down_first)
        grad_spread_back = to_features(grad_spread)
        added_back = jnp.einsum(
            "grpt,gpqr->pqt", grad_spread_back, up_first, preferred_element_type=jnp.float32
        )
        backward = (grads.astype(jnp.float32) + added_back).astype(jnp.bfloat16)
        total_first_up = total_first_up + jnp.einsum(
            "pqt,grpt->gpqr", stash_view, grad_spread_back, preferred_element_type=jnp.float32
        )
        total_second_up = total_second_up + jnp.einsum(
            "gprt,grot->grpo", spread_stash, grad_mixed, preferred_element_type=jnp.float32
        )
        total_first_down = total_first_down + jnp.einsum(
            "rot,prt->rop", hidden_stash, grad_arrived, preferred_element_type=jnp.float32
        )
        total_second_down = total_second_down + jnp.einsum(
            "rpt,pqt->prq", lowered_back, grads, preferred_element_type=jnp.float32
        )
        if tick_index + 1 < TICKS:
            moved_forward = from_behind(outputs, "section", 1)
            inputs = jnp.where(
                section_pos == 0,
                fresh_input.reshape(feature_blocks, FIRST_IN, tokens),
                moved_forward,
            )
            moved_backward = from_behind(backward, "section", -1)
            grads = jnp.where(
                section_pos == last_section,
                fresh_grad.reshape(feature_blocks, FIRST_IN, tokens),
                moved_backward,
            )
    factor = 1.0 / math.sqrt(TICKS * tokens)
    return (
        outputs.reshape(held_input.shape),
        backward.reshape(held_grad.shape),
        (total_first_up * factor).astype(jnp.bfloat16).reshape(first_up.shape),
        (total_second_up * factor).astype(jnp.bfloat16).reshape(second_up.shape),
        (total_first_down * factor).astype(jnp.bfloat16).reshape(first_down.shape),
        (total_second_down * factor).astype(jnp.bfloat16).reshape(second_down.shape),
    )


def solution(mesh):
    return jax.shard_map(
        shards,
        mesh=mesh,
        in_specs=(
            P("section", "blk", None),
            P("blk", None),
            P("section", None, "blk", None),
            P("section", "blk", None),
            P("blk", None),
            P("section", None, "blk", None),
            P("section", None, "blk", None),
            P("section", "blk", None),
            P("section", "blk", None),
        ),
        out_specs=(
            P("section", "blk", None),
            P("section", "blk", None),
            P("section", None, "blk", None),
            P("section", None, "blk", None),
            P("section", "blk", None),
            P("section", "blk", None),
        ),
        check_vma=False,
    )
```

profile of v0, /device:TPU:224, one launch (start us, length us, event | category | flops | bytes accessed | tf_op | source)
XLA Modules:
  0.0 197.9 jit_solution(12979514578403921260)
XLA Ops:
  0.6 1.4 reshape_squeeze.25
  4.7 7.0 %all-to-all-start = ((bf16[2,8,160,128]{3,0,1,2:T(2,128)(2,1)}), bf16[2,8,160,128]{3,0,1,2:T(2,128)(2,1)S(1)}, u32[]{:S(2)}, u32[]{:S(2)}) async-start(bf16[2,8,160,128]{3,0,1,2:T(2,128)(2,1)} %copy.186), calls=%async_computation | async-start | bytes 1310720 | tf_op jit(solution)/shard_map/all_to_all | solution.py:21
  12.2 1.3 copy.212
  13.5 11.1 %all-to-all-done = bf16[2,8,160,128]{3,0,1,2:T(2,128)(2,1)S(1)} async-done(((bf16[2,8,160,128]{3,0,1,2:T(2,128)(2,1)}), bf16[2,8,160,128]{3,0,1,2:T(2,128)(2,1)S(1)}, u32[]{:S(2)}, u32[]{:S(2)}) %all-to-all-start) | async-done | bytes 655392 | tf_op jit(solution)/shard_map/all_to_all | solution.py:21
  24.6 4.3 %all-to-all-start.5 = ((bf16[2,8,160,128]{3,0,1,2:T(2,128)(2,1)}), bf16[2,8,160,128]{3,0,1,2:T(2,128)(2,1)}, u32[]{:S(2)}, u32[]{:S(2)}) async-start(bf16[2,8,160,128]{3,0,1,2:T(2,128)(2,1)} %copy.212), calls=%async_computation.5 | async-start | bytes 1310720 | tf_op jit(solution)/shard_map/all_to_all | solution.py:21
  32.6 1.4 copy.228
  34.1 6.6 %all-to-all-done.5 = bf16[2,8,160,128]{3,0,1,2:T(2,128)(2,1)} async-done(((bf16[2,8,160,128]{3,0,1,2:T(2,128)(2,1)}), bf16[2,8,160,128]{3,0,1,2:T(2,128)(2,1)}, u32[]{:S(2)}, u32[]{:S(2)}) %all-to-all-start.5) | async-done | bytes 655392 | tf_op jit(solution)/shard_map/all_to_all | solution.py:21
  40.7 3.5 %all-to-all-start.4 = ((bf16[1,8,160,128]{3,1,0,2:T(8,128)(2,1)}), bf16[1,8,160,128]{3,1,0,2:T(8,128)(2,1)S(1)}, u32[]{:S(2)}, u32[]{:S(2)}) async-start(bf16[1,8,160,128]{3,1,0,2:T(8,128)(2,1)} %copy.208), calls=%async_computation.4 | async-start | bytes 655360 | tf_op jit(solution)/shard_map/all_to_all | solution.py:21
  44.3 1.5 convolution_bitcast_fusion.3
  46.9 1.4 convolution_bitcast_fusion.1
  48.4 4.9 %all-to-all-done.4 = bf16[1,8,160,128]{3,1,0,2:T(8,128)(2,1)S(1)} async-done(((bf16[1,8,160,128]{3,1,0,2:T(8,128)(2,1)}), bf16[1,8,160,128]{3,1,0,2:T(8,128)(2,1)S(1)}, u32[]{:S(2)}, u32[]{:S(2)}) %all-to-all-start.4) | async-done | bytes 327712 | tf_op jit(solution)/shard_map/all_to_all | solution.py:21
  54.1 3.6 %all-to-all-start.8 = ((bf16[2,8,160,128]{3,0,1,2:T(2,128)(2,1)}), bf16[2,8,160,128]{3,0,1,2:T(2,128)(2,1)S(1)}, u32[]{:S(2)}, u32[]{:S(2)}) async-start(bf16[2,8,160,128]{3,0,1,2:T(2,128)(2,1)} %copy.228), calls=%async_computation.8 | async-start | bytes 1310720 | tf_op jit(solution)/shard_map/all_to_all | solution.py:21
  57.7 2.3 %fusion.12 = bf16[1,10,128,128]{2,3,1,0:T(8,128)(2,1)} fusion(f32[2,10,128,128]{2,3,1,0:T(8,128)} %convolution_bitcast_fusion.3, bf16[16,128,128]{2,1,0:T(8,128)(2,1)S(1)} %bitcast.294), kind=kOutput, calls=%fused_computation.33 | convolution fusion | flops 43089920 | bytes 1966080 | tf_op jit(solution)/shard_map/rot,rop->rpt/dot_general | solution.py:37
  60.0 2.2 %copy.191 = bf16[1,10,128,128]{3,1,0,2:T(8,128)(2,1)} copy(bf16[1,10,128,128]{2,3,1,0:T(8,128)(2,1)} %fusion.12) | data formatting | bytes 655360 | tf_op jit(solution)/shard_map/broadcast_in_dim | solution.py:98
  62.1 2.7 %fusion.61 = (bf16[1,10,128,128]{2,3,1,0:T(8,128)(2,1)S(1)}, bf16[1,10,128,128]{2,3,1,0:T(8,128)(2,1)S(1)}, bf16[10,128,128]{1,2,0:T(8,128)(2,1)}) fusion(f32[2,10,128,128]{2,3,1,0:T(8,128)} %convolution_bitcast_fusion.1, bf16[16,128,128]{2,1,0:T(8,128)(2,1)S(1)} %bitcast.295, bf16[1,16,8,10,128]{4,2,3,1,0:T(8,128)(2,1)} %bitcast.308), kind=kOutput, calls=%fused_computation.109 | convolution fusion | flops 44564480 | bytes 2949120 | tf_op jit(solution)/shard_map/prt,rop->rot/dot_general | solution.py:49
  65.6 1.4 fusion.2
  67.1 1.4 all-to-all-done.8
  68.5 5.8 %all-to-all-start.1 = ((bf16[1,10,128,128]{3,1,0,2:T(8,128)(2,1)}), bf16[1,10,128,128]{3,1,0,2:T(8,128)(2,1)}, u32[]{:S(2)}, u32[]{:S(2)}) async-start(bf16[1,10,128,128]{3,1,0,2:T(8,128)(2,1)} %copy.191), calls=%async_computation.1 | async-start | bytes 1048576 | tf_op jit(solution)/shard_map/all_to_all | solution.py:25
  74.3 1.9 fusion.14
  76.2 2.2 %copy.246 = bf16[1,10,128,128]{3,1,0,2:T(8,128)(2,1)} copy(bf16[1,10,128,128]{2,3,1,0:T(8,128)(2,1)} %fusion.14) | data formatting | bytes 655360 | tf_op jit(solution)/shard_map/broadcast_in_dim | solution.py:101
  78.4 1.4 fusion.31
  79.8 4.7 %all-to-all-done.1 = bf16[1,10,128,128]{3,1,0,2:T(8,128)(2,1)} async-done(((bf16[1,10,128,128]{3,1,0,2:T(8,128)(2,1)}), bf16[1,10,128,128]{3,1,0,2:T(8,128)(2,1)}, u32[]{:S(2)}, u32[]{:S(2)}) %all-to-all-start.1) | async-done | bytes 327712 | tf_op jit(solution)/shard_map/all_to_all | solution.py:25
  84.5 4.2 %all-to-all-start.10 = ((bf16[1,10,128,128]{3,1,0,2:T(8,128)(2,1)}), bf16[1,10,128,128]{3,1,0,2:T(8,128)(2,1)}, u32[]{:S(2)}, u32[]{:S(2)}) async-start(bf16[1,10,128,128]{3,1,0,2:T(8,128)(2,1)} %copy.246), calls=%async_computation.10 | async-start | bytes 1048576 | tf_op jit(solution)/shard_map/all_to_all | solution.py:25
  88.7 2.3 %fusion.49 = f32[10,128,128]{2,1,0:T(8,128)} fusion(bf16[10,128,128]{1,2,0:T(8,128)(2,1)} %get-tuple-element.35, bf16[1,16,8,10,128]{4,2,3,1,0:T(8,128)(2,1)} %bitcast.309), kind=kOutput, calls=%fused_computation.95 | convolution fusion | flops 41943040 | bytes 1310720 | tf_op jit(solution)/shard_map/rot,prt->rop/dot_general | solution.py:115
  91.0 1.9 copy.218
  94.1 1.5 convolution_bitcast_fusion
  97.5 1.4 all-to-all-done.10
  98.9 5.8 %all-to-all-start.6 = ((bf16[2,10,128,128]{3,0,1,2:T(2,128)(2,1)}), bf16[2,10,128,128]{3,0,1,2:T(2,128)(2,1)}, u32[]{:S(2)}, u32[]{:S(2)}) async-start(bf16[2,10,128,128]{3,0,1,2:T(2,128)(2,1)} %copy.218), calls=%async_computation.6 | async-start | bytes 1310720 | tf_op jit(solution)/shard_map/all_to_all | solution.py:25
  106.0 2.2 %collective-permute-start = (bf16[8,40,128]{2,1,0:T(8,128)(2,1)S(1)}, bf16[8,40,128]{2,1,0:T(8,128)(2,1)S(1)}, u32[]{:S(2)}, u32[]{:S(2)}) collective-permute-start(bf16[8,40,128]{2,1,0:T(8,128)(2,1)S(1)} %fusion.24), channel_id=1, source_target_pairs={{0,16},{16,32},{32,48},{48,64},{64,80},{80,96},{96,112},{112,128},... | collective-permute-start | bytes 245768 | tf_op jit(solution)/shard_map/ppermute | solution.py:17
  110.5 1.4 collective-permute-done
  115.6 5.9 %all-to-all-start.2 = ((bf16[2,8,160,128]{3,0,1,2:T(2,128)(2,1)}), bf16[2,8,160,128]{3,0,1,2:T(2,128)(2,1)}, u32[]{:S(2)}, u32[]{:S(2)}) async-start(bf16[2,8,160,128]{3,0,1,2:T(2,128)(2,1)} %copy.197), calls=%async_computation.2 | async-start | bytes 1310720 | tf_op jit(solution)/shard_map/all_to_all | solution.py:21
  123.2 2.0 %collective-permute-start.1 = (bf16[8,40,128]{2,1,0:T(8,128)(2,1)S(1)}, bf16[8,40,128]{2,1,0:T(8,128)(2,1)S(1)}, u32[]{:S(2)}, u32[]{:S(2)}) collective-permute-start(bf16[8,40,128]{2,1,0:T(8,128)(2,1)S(1)} %fusion.23), channel_id=1, source_target_pairs={{16,0},{32,16},{48,32},{64,48},{80,64},{96,80},{112,96},{128,112},... | collective-permute-start | bytes 245768 | tf_op jit(solution)/shard_map/ppermute | solution.py:17
  125.2 1.4 fusion.42
  128.6 6.7 %all-to-all-done.2 = bf16[2,8,160,128]{3,0,1,2:T(2,128)(2,1)} async-done(((bf16[2,8,160,128]{3,0,1,2:T(2,128)(2,1)}), bf16[2,8,160,128]{3,0,1,2:T(2,128)(2,1)}, u32[]{:S(2)}, u32[]{:S(2)}) %all-to-all-start.2) | async-done | bytes 655392 | tf_op jit(solution)/shard_map/all_to_all | solution.py:21
  135.3 4.2 %all-to-all-start.7 = ((bf16[1,8,160,128]{3,1,0,2:T(8,128)(2,1)}), bf16[1,8,160,128]{3,1,0,2:T(8,128)(2,1)}, u32[]{:S(2)}, u32[]{:S(2)}) async-start(bf16[1,8,160,128]{3,1,0,2:T(8,128)(2,1)} %copy.224), calls=%async_computation.7 | async-start | bytes 655360 | tf_op jit(solution)/shard_map/all_to_all | solution.py:21
  142.8 2.2 %copy.202 = bf16[1,10,128,128]{3,1,0,2:T(8,128)(2,1)} copy(bf16[1,10,128,128]{2,3,1,0:T(8,128)(2,1)} %fusion.13) | data formatting | bytes 655360 | tf_op jit(solution)/shard_map/broadcast_in_dim | solution.py:98
  144.9 4.9 %all-to-all-done.7 = bf16[1,8,160,128]{3,1,0,2:T(8,128)(2,1)} async-done(((bf16[1,8,160,128]{3,1,0,2:T(8,128)(2,1)}), bf16[1,8,160,128]{3,1,0,2:T(8,128)(2,1)}, u32[]{:S(2)}, u32[]{:S(2)}) %all-to-all-start.7) | async-done | bytes 327712 | tf_op jit(solution)/shard_map/all_to_all | solution.py:21
  149.8 4.2 %all-to-all-start.3 = ((bf16[1,10,128,128]{3,1,0,2:T(8,128)(2,1)}), bf16[1,10,128,128]{3,1,0,2:T(8,128)(2,1)}, u32[]{:S(2)}, u32[]{:S(2)}) async-start(bf16[1,10,128,128]{3,1,0,2:T(8,128)(2,1)} %copy.202), calls=%async_computation.3 | async-start | bytes 1048576 | tf_op jit(solution)/shard_map/all_to_all | solution.py:25
  154.1 3.0 %fusion.62 = (bf16[1,10,128,128]{2,3,1,0:T(8,128)(2,1)}, bf16[1,10,128,128]{2,3,1,0:T(8,128)(2,1)}, bf16[10,128,128]{1,2,0:T(8,128)(2,1)S(1)}) fusion(f32[2,10,128,128]{2,3,1,0:T(8,128)} %convolution_bitcast_fusion, bf16[16,128,128]{2,1,0:T(8,128)(2,1)} %bitcast.297, bf16[1,16,8,10,128]{4,2,3,1,0:T(8,128)(2,1)} %bitcast.62), kind=kOutput, calls=%fused_computation.110 | convolution fusion | flops 44564480 | bytes 2949120 | tf_op jit(solution)/shard_map/prt,rop->rot/dot_general | solution.py:49
  158.7 2.2 %copy.250 = bf16[1,10,128,128]{3,1,0,2:T(8,128)(2,1)} copy(bf16[1,10,128,128]{2,3,1,0:T(8,128)(2,1)} %fusion.15) | data formatting | bytes 655360 | tf_op jit(solution)/shard_map/broadcast_in_dim | solution.py:101
  160.9 4.5 %all-to-all-done.3 = bf16[1,10,128,128]{3,1,0,2:T(8,128)(2,1)} async-done(((bf16[1,10,128,128]{3,1,0,2:T(8,128)(2,1)}), bf16[1,10,128,128]{3,1,0,2:T(8,128)(2,1)}, u32[]{:S(2)}, u32[]{:S(2)}) %all-to-all-start.3) | async-done | bytes 327712 | tf_op jit(solution)/shard_map/all_to_all | solution.py:25
  165.4 4.2 %all-to-all-start.11 = ((bf16[1,10,128,128]{3,1,0,2:T(8,128)(2,1)}), bf16[1,10,128,128]{3,1,0,2:T(8,128)(2,1)}, u32[]{:S(2)}, u32[]{:S(2)}) async-start(bf16[1,10,128,128]{3,1,0,2:T(8,128)(2,1)} %copy.250), calls=%async_computation.11 | async-start | bytes 1048576 | tf_op jit(solution)/shard_map/all_to_all | solution.py:25
  169.6 2.5 %fusion.3 = bf16[2,10,128,128]{2,3,1,0:T(8,128)(2,1)} fusion(bf16[1,10,128,128]{2,3,1,0:T(8,128)(2,1)} %get-tuple-element.31, bf16[1,10,128,128]{2,3,1,0:T(8,128)(2,1)} %get-tuple-element.30, bf16[2,10,128,128]{3,2,0,1:T(8,128)(2,1)S(1)} %reshape_squeeze.26), kind=kOutput, calls=%fused_computation.14 | convolution fusion | flops 84541440 | bytes 1966080 | tf_op jit(solution)/shard_map/grot,grpo->grpt/dot_general | solution.py:57
  172.1 3.0 %copy.234 = bf16[2,10,128,128]{3,0,1,2:T(2,128)(2,1)} copy(bf16[2,10,128,128]{2,3,1,0:T(8,128)(2,1)} %fusion.3) | data formatting | bytes 1310720 | tf_op jit(solution)/shard_map/convert_element_type | solution.py:59
  176.3 3.8 %all-to-all-done.11 = bf16[1,10,128,128]{3,1,0,2:T(8,128)(2,1)} async-done(((bf16[1,10,128,128]{3,1,0,2:T(8,128)(2,1)}), bf16[1,10,128,128]{3,1,0,2:T(8,128)(2,1)}, u32[]{:S(2)}, u32[]{:S(2)}) %all-to-all-start.11) | async-done | bytes 327712 | tf_op jit(solution)/shard_map/all_to_all | solution.py:25
  180.1 3.6 %all-to-all-start.9 = ((bf16[2,10,128,128]{3,0,1,2:T(2,128)(2,1)}), bf16[2,10,128,128]{3,0,1,2:T(2,128)(2,1)S(1)}, u32[]{:S(2)}, u32[]{:S(2)}) async-start(bf16[2,10,128,128]{3,0,1,2:T(2,128)(2,1)} %copy.234), calls=%async_computation.9 | async-start | bytes 1310720 | tf_op jit(solution)/shard_map/all_to_all | solution.py:25
  183.7 1.4 fusion.10
  192.2 2.7 %all-to-all-done.9 = bf16[2,10,128,128]{3,0,1,2:T(2,128)(2,1)S(1)} async-done(((bf16[2,10,128,128]{3,0,1,2:T(2,128)(2,1)}), bf16[2,10,128,128]{3,0,1,2:T(2,128)(2,1)S(1)}, u32[]{:S(2)}, u32[]{:S(2)}) %all-to-all-start.9) | async-done | bytes 655392 | tf_op jit(solution)/shard_map/all_to_all | solution.py:25
  (103 shorter events, 39.6 us)
Async XLA Ops:
  3.3 8.4 %copy-start.23 = (bf16[1,2,320,128]{3,2,1,0:T(8,128)(2,1)S(1)}, bf16[1,2,320,128]{3,2,1,0:T(8,128)(2,1)}, u32[]{:S(2)}) copy-start(bf16[1,2,320,128]{3,2,1,0:T(8,128)(2,1)} %param.11) | copy-start | bytes 491524
  4.7 20.0 %all-to-all-start = ((bf16[2,8,160,128]{3,0,1,2:T(2,128)(2,1)}), bf16[2,8,160,128]{3,0,1,2:T(2,128)(2,1)S(1)}, u32[]{:S(2)}, u32[]{:S(2)}) async-start(bf16[2,8,160,128]{3,0,1,2:T(2,128)(2,1)} %copy.186), calls=%async_computation | async-start | bytes 1310720 | tf_op jit(solution)/shard_map/all_to_all | solution.py:21
  12.2 16.8 %copy-start.24 = (bf16[1,8,6400]{2,1,0:T(8,128)(2,1)S(1)}, bf16[1,8,6400]{2,1,0:T(8,128)(2,1)}, u32[]{:S(2)}) copy-start(bf16[1,8,6400]{2,1,0:T(8,128)(2,1)} %param.17) | copy-start | bytes 307204
  12.2 17.3 %copy-start.10 = (bf16[1,2,10,16384]{3,1,2,0:T(2,128)(2,1)S(1)}, bf16[1,2,10,16384]{3,1,2,0:T(2,128)(2,1)}, u32[]{:S(2)}) copy-start(bf16[1,2,10,16384]{3,1,2,0:T(2,128)(2,1)} %param.15) | copy-start | bytes 1966084
  24.6 16.1 %all-to-all-start.5 = ((bf16[2,8,160,128]{3,0,1,2:T(2,128)(2,1)}), bf16[2,8,160,128]{3,0,1,2:T(2,128)(2,1)}, u32[]{:S(2)}, u32[]{:S(2)}) async-start(bf16[2,8,160,128]{3,0,1,2:T(2,128)(2,1)} %copy.212), calls=%async_computation.5 | async-start | bytes 1310720 | tf_op jit(solution)/shard_map/all_to_all | solution.py:21
  28.9 2.2 %copy-start.20 = (bf16[1,320,128]{2,1,0:T(8,128)(2,1)S(1)}, bf16[1,320,128]{2,1,0:T(8,128)(2,1)}, u32[]{:S(2)}) copy-start(bf16[1,320,128]{2,1,0:T(8,128)(2,1)} %param.12) | copy-start | bytes 245764
  31.1 43.1 %copy-start = (bf16[2,8,128,128]{3,2,1,0:T(8,128)(2,1)}, bf16[2,8,128,128]{3,2,1,0:T(8,128)(2,1)S(1)}, u32[]{:S(2)}) copy-start(bf16[2,8,128,128]{3,2,1,0:T(8,128)(2,1)S(1)} %copy.276) | copy-start | bytes 1572868
  40.7 12.6 %all-to-all-start.4 = ((bf16[1,8,160,128]{3,1,0,2:T(8,128)(2,1)}), bf16[1,8,160,128]{3,1,0,2:T(8,128)(2,1)S(1)}, u32[]{:S(2)}, u32[]{:S(2)}) async-start(bf16[1,8,160,128]{3,1,0,2:T(8,128)(2,1)} %copy.208), calls=%async_computation.4 | async-start | bytes 655360 | tf_op jit(solution)/shard_map/all_to_all | solution.py:21
  53.3 0.8 copy-start.8
  54.1 14.4 %all-to-all-start.8 = ((bf16[2,8,160,128]{3,0,1,2:T(2,128)(2,1)}), bf16[2,8,160,128]{3,0,1,2:T(2,128)(2,1)S(1)}, u32[]{:S(2)}, u32[]{:S(2)}) async-start(bf16[2,8,160,128]{3,0,1,2:T(2,128)(2,1)} %copy.228), calls=%async_computation.8 | async-start | bytes 1310720 | tf_op jit(solution)/shard_map/all_to_all | solution.py:21
  64.8 0.7 copy-start.18
  64.8 0.8 copy-start.19
  68.5 7.8 %copy-start.5 = (bf16[2,8,160,128]{3,0,1,2:T(2,128)(2,1)}, bf16[2,8,160,128]{3,0,1,2:T(2,128)(2,1)S(1)}, u32[]{:S(2)}) copy-start(bf16[2,8,160,128]{3,0,1,2:T(2,128)(2,1)S(1)} %all-to-all-done.8) | copy-start | bytes 1966084
  68.5 16.0 %all-to-all-start.1 = ((bf16[1,10,128,128]{3,1,0,2:T(8,128)(2,1)}), bf16[1,10,128,128]{3,1,0,2:T(8,128)(2,1)}, u32[]{:S(2)}, u32[]{:S(2)}) async-start(bf16[1,10,128,128]{3,1,0,2:T(8,128)(2,1)} %copy.191), calls=%async_computation.1 | async-start | bytes 1048576 | tf_op jit(solution)/shard_map/all_to_all | solution.py:25
  79.8 11.3 %copy-start.11 = (bf16[2,10,128,128]{2,3,1,0:T(8,128)(2,1)S(1)}, bf16[2,10,128,128]{2,3,1,0:T(8,128)(2,1)}, u32[]{:S(2)}) copy-start(bf16[2,10,128,128]{2,3,1,0:T(8,128)(2,1)} %fusion.2) | copy-start | bytes 1966084
  84.5 14.4 %all-to-all-start.10 = ((bf16[1,10,128,128]{3,1,0,2:T(8,128)(2,1)}), bf16[1,10,128,128]{3,1,0,2:T(8,128)(2,1)}, u32[]{:S(2)}, u32[]{:S(2)}) async-start(bf16[1,10,128,128]{3,1,0,2:T(8,128)(2,1)} %copy.246), calls=%async_computation.10 | async-start | bytes 1048576 | tf_op jit(solution)/shard_map/all_to_all | solution.py:25
  95.6 9.1 %copy-start.12 = (bf16[1,320,128]{2,1,0:T(8,128)(2,1)S(1)}, bf16[1,320,128]{2,1,0:T(8,128)(2,1)}, u32[]{:S(2)}) copy-start(bf16[1,320,128]{2,1,0:T(8,128)(2,1)} %param.9) | copy-start | bytes 245764
  98.9 16.7 %all-to-all-start.6 = ((bf16[2,10,128,128]{3,0,1,2:T(2,128)(2,1)}), bf16[2,10,128,128]{3,0,1,2:T(2,128)(2,1)}, u32[]{:S(2)}, u32[]{:S(2)}) async-start(bf16[2,10,128,128]{3,0,1,2:T(2,128)(2,1)} %copy.218), calls=%async_computation.6 | async-start | bytes 1310720 | tf_op jit(solution)/shard_map/all_to_all | solution.py:25
  104.7 4.8 %copy-start.21 = (bf16[1,320,128]{2,1,0:T(8,128)(2,1)S(1)}, bf16[1,320,128]{2,1,0:T(8,128)(2,1)}, u32[]{:S(2)}) copy-start(bf16[1,320,128]{2,1,0:T(8,128)(2,1)} %param.12) | copy-start | bytes 245764
  106.0 6.5 %copy-start.13 = (bf16[320,128]{1,0:T(8,128)(2,1)S(1)}, bf16[320,128]{1,0:T(8,128)(2,1)}, u32[]{:S(2)}) copy-start(bf16[320,128]{1,0:T(8,128)(2,1)} %param.10) | copy-start | bytes 245764
  106.0 5.9 %collective-permute-start = (bf16[8,40,128]{2,1,0:T(8,128)(2,1)S(1)}, bf16[8,40,128]{2,1,0:T(8,128)(2,1)S(1)}, u32[]{:S(2)}, u32[]{:S(2)}) collective-permute-start(bf16[8,40,128]{2,1,0:T(8,128)(2,1)S(1)} %fusion.24), channel_id=1, source_target_pairs={{0,16},{16,32},{32,48},{48,64},{64,80},{80,96},{96,112},{112,128},... | collective-permute-start | bytes 245768 | tf_op jit(solution)/shard_map/ppermute | solution.py:17
  111.9 0.6 copy-start.14
  115.6 19.8 %all-to-all-start.2 = ((bf16[2,8,160,128]{3,0,1,2:T(2,128)(2,1)}), bf16[2,8,160,128]{3,0,1,2:T(2,128)(2,1)}, u32[]{:S(2)}, u32[]{:S(2)}) async-start(bf16[2,8,160,128]{3,0,1,2:T(2,128)(2,1)} %copy.197), calls=%async_computation.2 | async-start | bytes 1310720 | tf_op jit(solution)/shard_map/all_to_all | solution.py:21
  121.5 1.4 copy-start.22
  122.9 4.6 %copy-start.25 = (bf16[320,128]{1,0:T(8,128)(2,1)S(1)}, bf16[320,128]{1,0:T(8,128)(2,1)}, u32[]{:S(2)}) copy-start(bf16[320,128]{1,0:T(8,128)(2,1)} %param.13) | copy-start | bytes 245764
  123.2 4.3 %collective-permute-start.1 = (bf16[8,40,128]{2,1,0:T(8,128)(2,1)S(1)}, bf16[8,40,128]{2,1,0:T(8,128)(2,1)S(1)}, u32[]{:S(2)}, u32[]{:S(2)}) collective-permute-start(bf16[8,40,128]{2,1,0:T(8,128)(2,1)S(1)} %fusion.23), channel_id=1, source_target_pairs={{16,0},{32,16},{48,32},{64,48},{80,64},{96,80},{112,96},{128,112},... | collective-permute-start | bytes 245768 | tf_op jit(solution)/shard_map/ppermute | solution.py:17
  135.3 14.5 %all-to-all-start.7 = ((bf16[1,8,160,128]{3,1,0,2:T(8,128)(2,1)}), bf16[1,8,160,128]{3,1,0,2:T(8,128)(2,1)}, u32[]{:S(2)}, u32[]{:S(2)}) async-start(bf16[1,8,160,128]{3,1,0,2:T(8,128)(2,1)} %copy.224), calls=%async_computation.7 | async-start | bytes 655360 | tf_op jit(solution)/shard_map/all_to_all | solution.py:21
  140.7 1.0 copy-start.1
  149.8 15.6 %all-to-all-start.3 = ((bf16[1,10,128,128]{3,1,0,2:T(8,128)(2,1)}), bf16[1,10,128,128]{3,1,0,2:T(8,128)(2,1)}, u32[]{:S(2)}, u32[]{:S(2)}) async-start(bf16[1,10,128,128]{3,1,0,2:T(8,128)(2,1)} %copy.202), calls=%async_computation.3 | async-start | bytes 1048576 | tf_op jit(solution)/shard_map/all_to_all | solution.py:25
  154.0 3.7 %copy-start.2 = (bf16[2,8,128,128]{3,2,1,0:T(8,128)(2,1)S(1)}, bf16[2,8,128,128]{3,2,1,0:T(8,128)(2,1)}, u32[]{:S(2)}) copy-start(bf16[2,8,128,128]{3,2,1,0:T(8,128)(2,1)} %copy-done) | copy-start | bytes 1572868
  157.0 0.7 copy-start.9
  165.4 14.8 %all-to-all-start.11 = ((bf16[1,10,128,128]{3,1,0,2:T(8,128)(2,1)}), bf16[1,10,128,128]{3,1,0,2:T(8,128)(2,1)}, u32[]{:S(2)}, u32[]{:S(2)}) async-start(bf16[1,10,128,128]{3,1,0,2:T(8,128)(2,1)} %copy.250), calls=%async_computation.11 | async-start | bytes 1048576 | tf_op jit(solution)/shard_map/all_to_all | solution.py:25
  172.1 3.0 %copy-start.16 = (bf16[1,10,128,128]{2,3,1,0:T(8,128)(2,1)S(1)}, bf16[1,10,128,128]{2,3,1,0:T(8,128)(2,1)}, u32[]{:S(2)}) copy-start(bf16[1,10,128,128]{2,3,1,0:T(8,128)(2,1)} %get-tuple-element.30) | copy-start | bytes 983044
  172.1 3.0 %copy-start.17 = (bf16[1,10,128,128]{2,3,1,0:T(8,128)(2,1)S(1)}, bf16[1,10,128,128]{2,3,1,0:T(8,128)(2,1)}, u32[]{:S(2)}) copy-start(bf16[1,10,128,128]{2,3,1,0:T(8,128)(2,1)} %get-tuple-element.31) | copy-start | bytes 983044
  176.3 7.4 %copy-start.3 = (f32[10,128,128]{2,1,0:T(8,128)S(1)}, f32[10,128,128]{2,1,0:T(8,128)}, u32[]{:S(2)}) copy-start(f32[10,128,128]{2,1,0:T(8,128)} %fusion.49) | copy-start | bytes 1966084
  176.3 8.9 %copy-start.6 = (bf16[2,10,128,128]{3,2,1,0:T(8,128)(2,1)S(1)}, bf16[2,10,128,128]{3,2,1,0:T(8,128)(2,1)}, u32[]{:S(2)}) copy-start(bf16[2,10,128,128]{3,2,1,0:T(8,128)(2,1)} %fusion.1) | copy-start | bytes 1966084
  180.1 14.8 %all-to-all-start.9 = ((bf16[2,10,128,128]{3,0,1,2:T(2,128)(2,1)}), bf16[2,10,128,128]{3,0,1,2:T(2,128)(2,1)S(1)}, u32[]{:S(2)}, u32[]{:S(2)}) async-start(bf16[2,10,128,128]{3,0,1,2:T(2,128)(2,1)} %copy.234), calls=%async_computation.9 | async-start | bytes 1310720 | tf_op jit(solution)/shard_map/all_to_all | solution.py:25
  187.2 2.5 %copy-start.7 = (f32[8,160,40]{1,2,0:T(8,128)S(1)}, f32[8,160,40]{1,2,0:T(8,128)}, u32[]{:S(2)}) copy-start(f32[8,160,40]{1,2,0:T(8,128)} %fusion.53) | copy-start | bytes 614404
  189.6 1.7 copy-start.15
  195.0 1.1 copy-start.4
where the time goes:
time: 200 us; the launch traced here: 198 us
  starting transfers between devices  60.7 us (30%)
  waiting for transfers between devices  56.3 us (28%)
  local copies, waits for them, and re-layouts  43.1 us (22%)
  matrix products  36.6 us (18%)
    all_to_all x6, waiting for transfers between devices, to_blocks(): lax.all_to_all(pieces, 'blk', split_axis=2, concat_axis=1, tiled=True)  35.6 us
    all_to_all x6, starting transfers between devices, to_blocks(): lax.all_to_all(pieces, 'blk', split_axis=2, concat_axis=1, tiled=True)  28.5 us
    all_to_all x6, starting transfers between devices, to_features(): lax.all_to_all(pieces, 'blk', split_axis=2, concat_axis=1, tiled=True)  27.9 us
    all_to_all x6, waiting for transfers between devices, to_features(): lax.all_to_all(pieces, 'blk', split_axis=2, concat_axis=1, tiled=True)  18.3 us
    all_to_all x12, local copies, waits for them, and re-layouts, to_features(): lax.all_to_all(pieces, 'blk', split_axis=2, concat_axis=1, tiled=True)  7.15 us
    dot_general x4, matrix products, middle(): jnp.einsum('rot,rop->rpt', hidden, down_first, preferred_element_type=jnp...  6.25 us
    dot_general x2, matrix products, backward_middle(): jnp.einsum('prt,rop->rot', grad_lowered, down_first, preferred_element_ty...  5.63 us
    unnamed x54, local copies, waits for them, and re-layouts  5.53 us
  transfers between devices with their start and end apart: 14, of which 14 were waited for; matrix products, arithmetic and copies ran while one was open for 35% of the time, Pallas kernels for 0%

commit v1 on v0

--- a/solution.py
+++ b/solution.py
@@ -22,7 +22,10 @@
 
 
 def to_features(pieces):
-    return lax.all_to_all(pieces, "blk", split_axis=2, concat_axis=1, tiled=True)
+    return jnp.concatenate(
+        lax.all_to_all(jnp.stack(jnp.split(pieces, lax.axis_size("blk"), axis=2)), "blk", 0, 0),
+        axis=1,
+    )
 
 
 def first_half(values, up_first):

time: 200 us -> 205 us (1.025)
  the two profiles are of different devices: /device:TPU:224 before, /device:TPU:96 now
where the time goes in v1:
time: 205 us; the launch traced here: 203 us
  starting transfers between devices  63.4 us (31%)
  local copies, waits for them, and re-layouts  55.8 us (27%)
  waiting for transfers between devices  51.6 us (25%)
  matrix products  30.4 us (15%)
    unnamed x148, local copies, waits for them, and re-layouts  32.9 us
    all_to_all x6, starting transfers between devices, to_features(): lax.all_to_all(jnp.stack(jnp.split(pieces, lax.axis_size('blk'), axis=2))...  30.6 us
    all_to_all x6, starting transfers between devices, to_blocks(): lax.all_to_all(pieces, 'blk', split_axis=2, concat_axis=1, tiled=True)  29 us
    all_to_all x6, waiting for transfers between devices, to_features(): lax.all_to_all(jnp.stack(jnp.split(pieces, lax.axis_size('blk'), axis=2))...  26.1 us
    all_to_all x6, waiting for transfers between devices, to_blocks(): lax.all_to_all(pieces, 'blk', split_axis=2, concat_axis=1, tiled=True)  23.1 us
    convert_element_type x4, local copies, waits for them, and re-layouts, first_half(): return jnp.einsum('pqt,gpqr->gprt', values, up_first, preferred_element_t...  5.42 us
    another operation x6, local copies, waits for them, and re-layouts, to_features(): jnp.stack(jnp.split(pieces, lax.axis_size('blk'), axis=2))  4.74 us
  transfers between devices with their start and end apart: 14, of which 12 were waited for; matrix products, arithmetic and copies ran while one was open for 37% of the time, Pallas kernels for 0%

profile of v1, /device:TPU:96, one launch (start us, length us, event | category | flops | bytes accessed | tf_op | source)
XLA Modules:
  0.0 202.7 jit_solution(2331002262014538120)
XLA Ops:
  0.6 1.4 reshape_squeeze.25
  2.0 1.3 fusion.6
  3.3 1.3 copy.123
  4.7 7.2 %all-to-all-start = ((bf16[2,8,160,128]{3,0,1,2:T(2,128)(2,1)}), bf16[2,8,160,128]{3,0,1,2:T(2,128)(2,1)S(1)}, u32[]{:S(2)}, u32[]{:S(2)}) async-start(bf16[2,8,160,128]{3,0,1,2:T(2,128)(2,1)} %copy.123), calls=%async_computation | async-start | bytes 1310720 | tf_op jit(solution)/shard_map/all_to_all | solution.py:21
  14.6 1.4 copy.147
  17.5 1.4 copy.162
  18.9 5.9 %all-to-all-done = bf16[2,8,160,128]{3,0,1,2:T(2,128)(2,1)S(1)} async-done(((bf16[2,8,160,128]{3,0,1,2:T(2,128)(2,1)}), bf16[2,8,160,128]{3,0,1,2:T(2,128)(2,1)S(1)}, u32[]{:S(2)}, u32[]{:S(2)}) %all-to-all-start) | async-done | bytes 655392 | tf_op jit(solution)/shard_map/all_to_all | solution.py:21
  24.8 3.6 %all-to-all-start.5 = ((bf16[2,8,160,128]{3,0,1,2:T(2,128)(2,1)}), bf16[2,8,160,128]{3,0,1,2:T(2,128)(2,1)S(1)}, u32[]{:S(2)}, u32[]{:S(2)}) async-start(bf16[2,8,160,128]{3,0,1,2:T(2,128)(2,1)} %copy.147), calls=%async_computation.5 | async-start | bytes 1310720 | tf_op jit(solution)/shard_map/all_to_all | solution.py:21
  38.4 2.1 %all-to-all-done.5 = bf16[2,8,160,128]{3,0,1,2:T(2,128)(2,1)S(1)} async-done(((bf16[2,8,160,128]{3,0,1,2:T(2,128)(2,1)}), bf16[2,8,160,128]{3,0,1,2:T(2,128)(2,1)S(1)}, u32[]{:S(2)}, u32[]{:S(2)}) %all-to-all-start.5) | async-done | bytes 655392 | tf_op jit(solution)/shard_map/all_to_all | solution.py:21
  40.5 5.1 %all-to-all-start.4 = ((bf16[1,8,160,128]{3,1,0,2:T(8,128)(2,1)}), bf16[1,8,160,128]{3,1,0,2:T(8,128)(2,1)}, u32[]{:S(2)}, u32[]{:S(2)}) async-start(bf16[1,8,160,128]{3,1,0,2:T(8,128)(2,1)} %copy.143), calls=%async_computation.4 | async-start | bytes 655360 | tf_op jit(solution)/shard_map/all_to_all | solution.py:21
  46.3 1.5 convolution_bitcast_fusion.1
  47.8 6.9 %all-to-all-done.4 = bf16[1,8,160,128]{3,1,0,2:T(8,128)(2,1)} async-done(((bf16[1,8,160,128]{3,1,0,2:T(8,128)(2,1)}), bf16[1,8,160,128]{3,1,0,2:T(8,128)(2,1)}, u32[]{:S(2)}, u32[]{:S(2)}) %all-to-all-start.4) | async-done | bytes 327712 | tf_op jit(solution)/shard_map/all_to_all | solution.py:21
  54.7 3.6 %all-to-all-start.8 = ((bf16[2,8,160,128]{3,0,1,2:T(2,128)(2,1)}), bf16[2,8,160,128]{3,0,1,2:T(2,128)(2,1)S(1)}, u32[]{:S(2)}, u32[]{:S(2)}) async-start(bf16[2,8,160,128]{3,0,1,2:T(2,128)(2,1)} %copy.162), calls=%async_computation.8 | async-start | bytes 1310720 | tf_op jit(solution)/shard_map/all_to_all | solution.py:21
  58.3 1.9 fusion.61
  71.8 2.2 %fusion.49 = f32[10,128,128]{2,1,0:T(8,128)} fusion(bf16[10,128,128]{1,2,0:T(8,128)(2,1)S(1)} %get-tuple-element.29, bf16[1,16,8,10,128]{4,2,3,1,0:T(8,128)(2,1)} %bitcast.67), kind=kOutput, calls=%fused_computation.93 | convolution fusion | flops 41943040 | bytes 1310720 | tf_op jit(solution)/shard_map/rot,prt->rop/dot_general | solution.py:118
  74.0 7.2 %all-to-all-start.1 = ((bf16[16,1,10,8,128]{4,3,2,1,0:T(8,128)(2,1)}), bf16[16,1,10,8,128]{4,3,2,1,0:T(8,128)(2,1)}, u32[]{:S(2)}, u32[]{:S(2)}) async-start(bf16[16,1,10,8,128]{4,3,2,1,0:T(8,128)(2,1)} %constant_dynamic-update-slice_fusion), calls=%async_computation.1 | async-start | bytes 655360 | tf_op jit(solution)/shard_map/all_to_all | solution.py:26
  81.2 1.3 constant_dynamic-update-slice_fusion.64
  82.6 1.4 fusion.31
  84.0 6.4 %all-to-all-done.1 = bf16[16,1,10,8,128]{4,3,2,1,0:T(8,128)(2,1)} async-done(((bf16[16,1,10,8,128]{4,3,2,1,0:T(8,128)(2,1)}), bf16[16,1,10,8,128]{4,3,2,1,0:T(8,128)(2,1)}, u32[]{:S(2)}, u32[]{:S(2)}) %all-to-all-start.1) | async-done | bytes 327712 | tf_op jit(solution)/shard_map/all_to_all | solution.py:26
  90.3 4.2 %all-to-all-start.10 = ((bf16[16,1,10,8,128]{4,3,2,1,0:T(8,128)(2,1)}), bf16[16,1,10,8,128]{4,3,2,1,0:T(8,128)(2,1)}, u32[]{:S(2)}, u32[]{:S(2)}) async-start(bf16[16,1,10,8,128]{4,3,2,1,0:T(8,128)(2,1)} %constant_dynamic-update-slice_fusion.64), calls=%async_computation.10 | async-start | bytes 655360 | tf_op jit(solution)/shard_map/all_to_all | solution.py:26
  94.5 1.4 constant_dynamic-update-slice_fusion.32
  95.9 1.2 copy.163
  97.1 1.5 convolution_bitcast_fusion
  98.6 5.0 %all-to-all-done.10 = bf16[16,1,10,8,128]{4,3,2,1,0:T(8,128)(2,1)} async-done(((bf16[16,1,10,8,128]{4,3,2,1,0:T(8,128)(2,1)}), bf16[16,1,10,8,128]{4,3,2,1,0:T(8,128)(2,1)}, u32[]{:S(2)}, u32[]{:S(2)}) %all-to-all-start.10) | async-done | bytes 327712 | tf_op jit(solution)/shard_map/all_to_all | solution.py:26
  103.6 4.3 %all-to-all-start.6 = ((bf16[16,2,10,8,128]{4,3,2,1,0:T(8,128)(2,1)}), bf16[16,2,10,8,128]{4,3,2,1,0:T(8,128)(2,1)}, u32[]{:S(2)}, u32[]{:S(2)}) async-start(bf16[16,2,10,8,128]{4,3,2,1,0:T(8,128)(2,1)} %constant_dynamic-update-slice_fusion.32), calls=%async_computation.6 | async-start | bytes 1310720 | tf_op jit(solution)/shard_map/all_to_all | solution.py:26
  107.9 1.3 fusion.24
  109.2 1.9 collective-permute-start
  111.1 2.0 %fusion.53 = f32[8,160,40]{1,2,0:T(8,128)} fusion(bf16[8,40,128]{2,1,0:T(8,128)(2,1)} %bitcast.672, bf16[160,8,128]{2,1,0:T(8,128)(2,1)} %bitcast.169), kind=kOutput, calls=%fused_computation.97 | convolution fusion | flops 13107200 | bytes 614400 | tf_op jit(solution)/shard_map/rpt,pqt->prq/dot_general | solution.py:121
  113.1 1.8 collective-permute-done
  115.3 1.3 copy.133
  116.7 2.0 %all-to-all-done.6 = bf16[16,2,10,8,128]{4,3,2,1,0:T(8,128)(2,1)} async-done(((bf16[16,2,10,8,128]{4,3,2,1,0:T(8,128)(2,1)}), bf16[16,2,10,8,128]{4,3,2,1,0:T(8,128)(2,1)}, u32[]{:S(2)}, u32[]{:S(2)}) %all-to-all-start.6) | async-done | bytes 655392 | tf_op jit(solution)/shard_map/all_to_all | solution.py:26
  118.7 5.3 %all-to-all-start.2 = ((bf16[2,8,160,128]{3,0,1,2:T(2,128)(2,1)}), bf16[2,8,160,128]{3,0,1,2:T(2,128)(2,1)}, u32[]{:S(2)}, u32[]{:S(2)}) async-start(bf16[2,8,160,128]{3,0,1,2:T(2,128)(2,1)} %copy.133), calls=%async_computation.2 | async-start | bytes 1310720 | tf_op jit(solution)/shard_map/all_to_all | solution.py:21
  125.5 1.9 collective-permute-start.1
  127.5 1.4 fusion.42
  130.6 8.2 %all-to-all-done.2 = bf16[2,8,160,128]{3,0,1,2:T(2,128)(2,1)} async-done(((bf16[2,8,160,128]{3,0,1,2:T(2,128)(2,1)}), bf16[2,8,160,128]{3,0,1,2:T(2,128)(2,1)}, u32[]{:S(2)}, u32[]{:S(2)}) %all-to-all-start.2) | async-done | bytes 655392 | tf_op jit(solution)/shard_map/all_to_all | solution.py:21
  138.8 4.2 %all-to-all-start.7 = ((bf16[1,8,160,128]{3,1,0,2:T(8,128)(2,1)}), bf16[1,8,160,128]{3,1,0,2:T(8,128)(2,1)}, u32[]{:S(2)}, u32[]{:S(2)}) async-start(bf16[1,8,160,128]{3,1,0,2:T(8,128)(2,1)} %copy.158), calls=%async_computation.7 | async-start | bytes 655360 | tf_op jit(solution)/shard_map/all_to_all | solution.py:21
  143.0 1.2 copy.134
  155.4 7.1 %all-to-all-start.3 = ((bf16[16,1,10,8,128]{4,3,2,1,0:T(8,128)(2,1)}), bf16[16,1,10,8,128]{4,3,2,1,0:T(8,128)(2,1)}, u32[]{:S(2)}, u32[]{:S(2)}) async-start(bf16[16,1,10,8,128]{4,3,2,1,0:T(8,128)(2,1)} %constant_dynamic-update-slice_fusion.16), calls=%async_computation.3 | async-start | bytes 655360 | tf_op jit(solution)/shard_map/all_to_all | solution.py:26
  162.5 2.1 %fusion.62 = (bf16[1,10,128,128]{2,3,1,0:T(8,128)(2,1)S(1)}, bf16[1,10,128,128]{2,3,1,0:T(8,128)(2,1)S(1)}, bf16[10,128,128]{1,2,0:T(8,128)(2,1)S(1)}) fusion(f32[2,10,128,128]{2,3,1,0:T(8,128)} %convolution_bitcast_fusion, bf16[16,128,128]{2,1,0:T(8,128)(2,1)} %bitcast.653, bf16[1,16,8,10,128]{4,2,3,1,0:T(8,128)(2,1)} %bitcast.107), kind=kOutput, calls=%fused_computation.104 | convolution fusion | flops 44564480 | bytes 2949120 | tf_op jit(solution)/shard_map/prt,rop->rot/dot_general | solution.py:52
  167.5 4.5 %all-to-all-done.3 = bf16[16,1,10,8,128]{4,3,2,1,0:T(8,128)(2,1)} async-done(((bf16[16,1,10,8,128]{4,3,2,1,0:T(8,128)(2,1)}), bf16[16,1,10,8,128]{4,3,2,1,0:T(8,128)(2,1)}, u32[]{:S(2)}, u32[]{:S(2)}) %all-to-all-start.3) | async-done | bytes 327712 | tf_op jit(solution)/shard_map/all_to_all | solution.py:26
  172.0 4.2 %all-to-all-start.11 = ((bf16[16,1,10,8,128]{4,3,2,1,0:T(8,128)(2,1)}), bf16[16,1,10,8,128]{4,3,2,1,0:T(8,128)(2,1)}, u32[]{:S(2)}, u32[]{:S(2)}) async-start(bf16[16,1,10,8,128]{4,3,2,1,0:T(8,128)(2,1)} %copy-done.16), calls=%async_computation.11 | async-start | bytes 655360 | tf_op jit(solution)/shard_map/all_to_all | solution.py:26
  177.8 2.2 %fusion.1 = bf16[2,10,128,128]{3,2,1,0:T(8,128)(2,1)} fusion(f32[2,10,128,128]{3,2,1,0:T(8,128)S(1)} %fusion.31, bf16[2,16,8,10,128]{4,2,3,1,0:T(8,128)(2,1)S(1)} %bitcast.649, bf16[1,10,128,128]{2,3,1,0:T(8,128)(2,1)} %copy-done.21, bf16[1,10,128,128]{2,3,1,0:T(8,128)(2,1)} %copy-done.20), kind=kOutput, calls=%fused_computation.6 | convolution fusion | flops 85196800 | bytes 3276800 | tf_op jit(solution)/shard_map/gprt,grot->grpo/dot_general | solution.py:115
  180.1 5.2 %all-to-all-done.11 = bf16[16,1,10,8,128]{4,3,2,1,0:T(8,128)(2,1)} async-done(((bf16[16,1,10,8,128]{4,3,2,1,0:T(8,128)(2,1)}), bf16[16,1,10,8,128]{4,3,2,1,0:T(8,128)(2,1)}, u32[]{:S(2)}, u32[]{:S(2)}) %all-to-all-start.11) | async-done | bytes 327712 | tf_op jit(solution)/shard_map/all_to_all | solution.py:26
  185.2 3.6 %all-to-all-start.9 = ((bf16[16,2,10,8,128]{4,3,2,1,0:T(8,128)(2,1)}), bf16[16,2,10,8,128]{4,3,2,1,0:T(8,128)(2,1)S(1)}, u32[]{:S(2)}, u32[]{:S(2)}) async-start(bf16[16,2,10,8,128]{4,3,2,1,0:T(8,128)(2,1)} %copy-done.11), calls=%async_computation.9 | async-start | bytes 1310720 | tf_op jit(solution)/shard_map/all_to_all | solution.py:26
  188.8 1.4 fusion.10
  192.3 1.3 fusion.20
  194.9 1.9 add_convert_fusion.1
  196.8 3.1 %all-to-all-done.9 = bf16[16,2,10,8,128]{4,3,2,1,0:T(8,128)(2,1)S(1)} async-done(((bf16[16,2,10,8,128]{4,3,2,1,0:T(8,128)(2,1)}), bf16[16,2,10,8,128]{4,3,2,1,0:T(8,128)(2,1)S(1)}, u32[]{:S(2)}, u32[]{:S(2)}) %all-to-all-start.9) | async-done | bytes 655392 | tf_op jit(solution)/shard_map/all_to_all | solution.py:26
  (187 shorter events, 51.6 us)
Async XLA Ops:
  3.3 8.5 %copy-start.26 = (bf16[1,8,6400]{2,1,0:T(8,128)(2,1)S(1)}, bf16[1,8,6400]{2,1,0:T(8,128)(2,1)}, u32[]{:S(2)}) copy-start(bf16[1,8,6400]{2,1,0:T(8,128)(2,1)} %param.17) | copy-start | bytes 307204
  3.3 9.1 %copy-start.14 = (bf16[1,2,10,16384]{3,1,2,0:T(2,128)(2,1)S(1)}, bf16[1,2,10,16384]{3,1,2,0:T(2,128)(2,1)}, u32[]{:S(2)}) copy-start(bf16[1,2,10,16384]{3,1,2,0:T(2,128)(2,1)} %param.15) | copy-start | bytes 1966084
  4.7 8.3 %copy-start.15 = (bf16[1,10,16384]{2,1,0:T(8,128)(2,1)S(1)}, bf16[1,10,16384]{2,1,0:T(8,128)(2,1)}, u32[]{:S(2)}) copy-start(bf16[1,10,16384]{2,1,0:T(8,128)(2,1)} %param.16) | copy-start | bytes 983044
  4.7 20.1 %all-to-all-start = ((bf16[2,8,160,128]{3,0,1,2:T(2,128)(2,1)}), bf16[2,8,160,128]{3,0,1,2:T(2,128)(2,1)S(1)}, u32[]{:S(2)}, u32[]{:S(2)}) async-start(bf16[2,8,160,128]{3,0,1,2:T(2,128)(2,1)} %copy.123), calls=%async_computation | async-start | bytes 1310720 | tf_op jit(solution)/shard_map/all_to_all | solution.py:21
  13.0 48.3 %copy-start = (bf16[2,8,128,128]{3,2,1,0:T(8,128)(2,1)}, bf16[2,8,128,128]{3,2,1,0:T(8,128)(2,1)S(1)}, u32[]{:S(2)}) copy-start(bf16[2,8,128,128]{3,2,1,0:T(8,128)(2,1)S(1)} %copy.217) | copy-start | bytes 1572868
  13.1 3.0 %copy-start.24 = (bf16[1,320,128]{2,1,0:T(8,128)(2,1)S(1)}, bf16[1,320,128]{2,1,0:T(8,128)(2,1)}, u32[]{:S(2)}) copy-start(bf16[1,320,128]{2,1,0:T(8,128)(2,1)} %param.12) | copy-start | bytes 245764
  24.8 15.7 %all-to-all-start.5 = ((bf16[2,8,160,128]{3,0,1,2:T(2,128)(2,1)}), bf16[2,8,160,128]{3,0,1,2:T(2,128)(2,1)S(1)}, u32[]{:S(2)}, u32[]{:S(2)}) async-start(bf16[2,8,160,128]{3,0,1,2:T(2,128)(2,1)} %copy.147), calls=%async_computation.5 | async-start | bytes 1310720 | tf_op jit(solution)/shard_map/all_to_all | solution.py:21
  40.5 14.2 %all-to-all-start.4 = ((bf16[1,8,160,128]{3,1,0,2:T(8,128)(2,1)}), bf16[1,8,160,128]{3,1,0,2:T(8,128)(2,1)}, u32[]{:S(2)}, u32[]{:S(2)}) async-start(bf16[1,8,160,128]{3,1,0,2:T(8,128)(2,1)} %copy.143), calls=%async_computation.4 | async-start | bytes 655360 | tf_op jit(solution)/shard_map/all_to_all | solution.py:21
  54.7 19.3 %all-to-all-start.8 = ((bf16[2,8,160,128]{3,0,1,2:T(2,128)(2,1)}), bf16[2,8,160,128]{3,0,1,2:T(2,128)(2,1)S(1)}, u32[]{:S(2)}, u32[]{:S(2)}) async-start(bf16[2,8,160,128]{3,0,1,2:T(2,128)(2,1)} %copy.162), calls=%async_computation.8 | async-start | bytes 1310720 | tf_op jit(solution)/shard_map/all_to_all | solution.py:21
  60.3 0.8 copy-start.22
  60.3 0.8 copy-start.23
  60.9 10.0 %copy-start.12 = (bf16[2,10,128,128]{3,2,1,0:T(8,128)(2,1)}, bf16[2,10,128,128]{3,2,1,0:T(8,128)(2,1)S(1)}, u32[]{:S(2)}) copy-start(bf16[2,10,128,128]{3,2,1,0:T(8,128)(2,1)S(1)} %fusion.2) | copy-start | bytes 1966084
  61.7 9.2 %copy-start.9 = (bf16[1,10,128,128]{3,2,1,0:T(8,128)(2,1)}, bf16[1,10,128,128]{3,2,1,0:T(8,128)(2,1)S(1)}, u32[]{:S(2)}) copy-start(bf16[1,10,128,128]{3,2,1,0:T(8,128)(2,1)S(1)} %fusion.14) | copy-start | bytes 983044
  71.0 0.8 copy-start.10
  74.0 7.2 %copy-start.5 = (bf16[2,8,160,128]{3,0,1,2:T(2,128)(2,1)}, bf16[2,8,160,128]{3,0,1,2:T(2,128)(2,1)S(1)}, u32[]{:S(2)}) copy-start(bf16[2,8,160,128]{3,0,1,2:T(2,128)(2,1)S(1)} %all-to-all-done.8) | copy-start | bytes 1966084
  74.0 16.3 %all-to-all-start.1 = ((bf16[16,1,10,8,128]{4,3,2,1,0:T(8,128)(2,1)}), bf16[16,1,10,8,128]{4,3,2,1,0:T(8,128)(2,1)}, u32[]{:S(2)}, u32[]{:S(2)}) async-start(bf16[16,1,10,8,128]{4,3,2,1,0:T(8,128)(2,1)} %constant_dynamic-update-slice_fusion), calls=%async_computation.1 | async-start | bytes 655360 | tf_op jit(solution)/shard_map/all_to_all | solution.py:26
  90.3 13.3 %all-to-all-start.10 = ((bf16[16,1,10,8,128]{4,3,2,1,0:T(8,128)(2,1)}), bf16[16,1,10,8,128]{4,3,2,1,0:T(8,128)(2,1)}, u32[]{:S(2)}, u32[]{:S(2)}) async-start(bf16[16,1,10,8,128]{4,3,2,1,0:T(8,128)(2,1)} %constant_dynamic-update-slice_fusion.64), calls=%async_computation.10 | async-start | bytes 655360 | tf_op jit(solution)/shard_map/all_to_all | solution.py:26
  98.6 9.3 %copy-start.17 = (bf16[1,320,128]{2,1,0:T(8,128)(2,1)S(1)}, bf16[1,320,128]{2,1,0:T(8,128)(2,1)}, u32[]{:S(2)}) copy-start(bf16[1,320,128]{2,1,0:T(8,128)(2,1)} %param.9) | copy-start | bytes 245764
  103.6 15.1 %all-to-all-start.6 = ((bf16[16,2,10,8,128]{4,3,2,1,0:T(8,128)(2,1)}), bf16[16,2,10,8,128]{4,3,2,1,0:T(8,128)(2,1)}, u32[]{:S(2)}, u32[]{:S(2)}) async-start(bf16[16,2,10,8,128]{4,3,2,1,0:T(8,128)(2,1)} %constant_dynamic-update-slice_fusion.32), calls=%async_computation.6 | async-start | bytes 1310720 | tf_op jit(solution)/shard_map/all_to_all | solution.py:26
  107.9 7.1 %copy-start.18 = (bf16[320,128]{1,0:T(8,128)(2,1)S(1)}, bf16[320,128]{1,0:T(8,128)(2,1)}, u32[]{:S(2)}) copy-start(bf16[320,128]{1,0:T(8,128)(2,1)} %param.10) | copy-start | bytes 245764
  109.2 5.8 %collective-permute-start = (bf16[8,40,128]{2,1,0:T(8,128)(2,1)S(1)}, bf16[8,40,128]{2,1,0:T(8,128)(2,1)S(1)}, u32[]{:S(2)}, u32[]{:S(2)}) collective-permute-start(bf16[8,40,128]{2,1,0:T(8,128)(2,1)S(1)} %fusion.24), channel_id=1, source_target_pairs={{0,16},{16,32},{32,48},{48,64},{64,80},{80,96},{96,112},{112,128},... | collective-permute-start | bytes 245768 | tf_op jit(solution)/shard_map/ppermute | solution.py:17
  118.7 20.1 %all-to-all-start.2 = ((bf16[2,8,160,128]{3,0,1,2:T(2,128)(2,1)}), bf16[2,8,160,128]{3,0,1,2:T(2,128)(2,1)}, u32[]{:S(2)}, u32[]{:S(2)}) async-start(bf16[2,8,160,128]{3,0,1,2:T(2,128)(2,1)} %copy.133), calls=%async_computation.2 | async-start | bytes 1310720 | tf_op jit(solution)/shard_map/all_to_all | solution.py:21
  124.0 1.2 copy-start.25
  125.2 4.3 %copy-start.27 = (bf16[320,128]{1,0:T(8,128)(2,1)S(1)}, bf16[320,128]{1,0:T(8,128)(2,1)}, u32[]{:S(2)}) copy-start(bf16[320,128]{1,0:T(8,128)(2,1)} %param.13) | copy-start | bytes 245764
  125.5 4.0 %collective-permute-start.1 = (bf16[8,40,128]{2,1,0:T(8,128)(2,1)S(1)}, bf16[8,40,128]{2,1,0:T(8,128)(2,1)S(1)}, u32[]{:S(2)}, u32[]{:S(2)}) collective-permute-start(bf16[8,40,128]{2,1,0:T(8,128)(2,1)S(1)} %fusion.23), channel_id=1, source_target_pairs={{16,0},{32,16},{48,32},{64,48},{80,64},{96,80},{112,96},{128,112},... | collective-permute-start | bytes 245768 | tf_op jit(solution)/shard_map/ppermute | solution.py:17
  138.8 16.5 %all-to-all-start.7 = ((bf16[1,8,160,128]{3,1,0,2:T(8,128)(2,1)}), bf16[1,8,160,128]{3,1,0,2:T(8,128)(2,1)}, u32[]{:S(2)}, u32[]{:S(2)}) async-start(bf16[1,8,160,128]{3,1,0,2:T(8,128)(2,1)} %copy.158), calls=%async_computation.7 | async-start | bytes 655360 | tf_op jit(solution)/shard_map/all_to_all | solution.py:21
  144.2 1.0 copy-start.1
  155.4 16.6 %all-to-all-start.3 = ((bf16[16,1,10,8,128]{4,3,2,1,0:T(8,128)(2,1)}), bf16[16,1,10,8,128]{4,3,2,1,0:T(8,128)(2,1)}, u32[]{:S(2)}, u32[]{:S(2)}) async-start(bf16[16,1,10,8,128]{4,3,2,1,0:T(8,128)(2,1)} %constant_dynamic-update-slice_fusion.16), calls=%async_computation.3 | async-start | bytes 655360 | tf_op jit(solution)/shard_map/all_to_all | solution.py:26
  164.6 0.8 copy-start.20
  164.6 0.9 copy-start.21
  164.6 1.1 copy-start.8
  164.6 1.4 copy-start.2
  165.2 1.5 copy-start.13
  166.7 0.7 copy-start.16
  172.0 13.3 %all-to-all-start.11 = ((bf16[16,1,10,8,128]{4,3,2,1,0:T(8,128)(2,1)}), bf16[16,1,10,8,128]{4,3,2,1,0:T(8,128)(2,1)}, u32[]{:S(2)}, u32[]{:S(2)}) async-start(bf16[16,1,10,8,128]{4,3,2,1,0:T(8,128)(2,1)} %copy-done.16), calls=%async_computation.11 | async-start | bytes 655360 | tf_op jit(solution)/shard_map/all_to_all | solution.py:26
  177.0 0.9 copy-start.11
  180.1 8.8 %copy-start.3 = (f32[10,128,128]{2,1,0:T(8,128)S(1)}, f32[10,128,128]{2,1,0:T(8,128)}, u32[]{:S(2)}) copy-start(f32[10,128,128]{2,1,0:T(8,128)} %fusion.49) | copy-start | bytes 1966084
  180.1 10.2 %copy-start.6 = (bf16[2,10,128,128]{3,2,1,0:T(8,128)(2,1)S(1)}, bf16[2,10,128,128]{3,2,1,0:T(8,128)(2,1)}, u32[]{:S(2)}) copy-start(bf16[2,10,128,128]{3,2,1,0:T(8,128)(2,1)} %fusion.1) | copy-start | bytes 1966084
  185.2 14.6 %all-to-all-start.9 = ((bf16[16,2,10,8,128]{4,3,2,1,0:T(8,128)(2,1)}), bf16[16,2,10,8,128]{4,3,2,1,0:T(8,128)(2,1)S(1)}, u32[]{:S(2)}, u32[]{:S(2)}) async-start(bf16[16,2,10,8,128]{4,3,2,1,0:T(8,128)(2,1)} %copy-done.11), calls=%async_computation.9 | async-start | bytes 1310720 | tf_op jit(solution)/shard_map/all_to_all | solution.py:26
  190.4 2.0 copy-start.7
  191.4 3.5 %copy-start.19 = (bf16[320,128]{1,0:T(8,128)(2,1)S(1)}, bf16[320,128]{1,0:T(8,128)(2,1)}, u32[]{:S(2)}) copy-start(bf16[320,128]{1,0:T(8,128)(2,1)} %param.10) | copy-start | bytes 245764
  199.9 1.1 copy-start.4
